TPU v7x, 256 devices: a whole 4x4x8 slice. The times are simulated.
256 devices in a mesh: level: 4 (over x), basin: 32 (over y, z), group: 2 (over core).
Axes of the slice: x: 4, y: 4, z: 8, core: 2. Of those that a mesh axis runs over, the one named last changes fastest.
Arguments:
- lateral: float32 [96, 131072], P('group', ('level', 'basin')), may hold values from 0.02 to 2
- cotangent: float32 [96, 131072], P('group', ('level', 'basin')), may hold values from -6 to 6
- attributes: float32 [16, 131072], P(None, ('level', 'basin')), may hold values from -6 to 6
- region: int32 [131072], P(('level', 'basin')), may hold values from 0 to 127
- feeders: int32 [2, 131072], P(None, ('level', 'basin')), may hold values from 0 to 1151
- feeder_count: int32 [131072], P(('level', 'basin')), may hold values from 0 to 2
- live_blocks: int32 [128], P(('level', 'basin')), may hold values from 1 to 8, as said below
- net_weight: float32 [128, 16, 2], replicated, may hold values from -1.5 to 1.5
Outputs:
- outflow: float32 [96, 131072], P('group', ('level', 'basin'))
- grad_net: float32 [128, 16, 2], P('basin')
Inputs may be any that keep to these rules, and one draw needn't show every extreme that they name: `feeders`: entries below 1024 name a reach slot of the same basin shard one level lower in the order; an entry e of 1024 or more names reach slot e - 1024 of the previous basin shard one level lower. Nothing feeds level 0, and the previous shard of basin shard 0 is empty. `live_blocks`: reach slots at or past 128 times this count are padding; some shard is full in every draw.
All inputs are finite; a program needn't handle non-finite values.
Results may differ from a plain program's by a relative error of at most 0.00029.
Values sent between devices are 32-bit elements; how exact they have to be, the bound alone decides.
No kernel may reach another device: no remote copies, remote signals or barrier semaphores. Data moves between devices by JAX's collectives and lax.ppermute only.
A program may use at most 64 MiB of HBM per device.

v0:
```python
import jax
import jax.numpy as jnp
from jax import lax
from jax.sharding import PartitionSpec as P

BLOCK = 128


def shifted(value, axis, steps):
    count = lax.axis_size(axis)
    leading, last = (max(0, -steps), min(count, count - steps))
    return lax.ppermute(value, axis, [(source, source + steps) for source in range(leading, last)])


def carried_in(value, axis, join, neutral, backward):
    count, mine = (lax.axis_size(axis), lax.axis_index(axis))
    pieces = lax.all_gather(value, axis)
    if backward:
        pieces = pieces[::-1]
        mine = count - 1 - mine
    subtotal = jnp.full_like(value, 0) + jnp.asarray(neutral, value.dtype)

    def turn(position, subtotal):
        longer = join(subtotal, pieces[position])
        return jnp.where(position < mine, longer, subtotal)

    return lax.fori_loop(0, count - 1, turn, subtotal)


def coefficients(raw_params):
    travel = 1.0 + 47.0 * jax.nn.sigmoid(raw_params[0])
    weighting = 0.05 + 0.4 * jax.nn.sigmoid(raw_params[1])
    storage = travel * (1.0 - weighting)
    divisor = storage + 0.5
    return (
        (0.5 - travel * weighting) / divisor,
        (0.5 + travel * weighting) / divisor,
        (storage - 0.5) / divisor,
        1.0 / divisor,
    )


def affine_join(earlier, latter):
    return (earlier[0] * latter[0], latter[0] * earlier[1] + latter[1])


def stack_affine(pair):
    return jnp.stack([pair[0], pair[1]], axis=0)


def split_affine(stacked):
    return (stacked[0], stacked[1])


def stacked_affine(earlier, latter):
    return stack_affine(affine_join(split_affine(earlier), split_affine(latter)))


def body(lateral, cotangent, attributes, region, feeders, feeder_count, live_blocks, net_weight):
    steps_dev, reach_dev = lateral.shape
    outlets = reach_dev // 8
    regions, attr_count, param_count = net_weight.shape
    levels = lax.axis_size("level")
    up_count = feeders.shape[0]
    slot_ids = lax.broadcasted_iota(jnp.int32, (reach_dev,), 0)
    live_mask = (slot_ids < live_blocks[0] * BLOCK).astype(jnp.float32)
    member_table = (
        region[None, :] == lax.broadcasted_iota(jnp.int32, (regions, reach_dev), 0)
    ).astype(jnp.float32)
    per_region = jnp.dot(
        jnp.transpose(net_weight, (0, 2, 1)).reshape(regions * param_count, attr_count),
        attributes,
        precision=lax.Precision.HIGHEST,
        preferred_element_type=jnp.float32,
    )
    raw_params = jnp.einsum(
        "rpi,ri->pi",
        per_region.reshape(regions, param_count, reach_dev),
        member_table,
        precision=lax.Precision.HIGHEST,
    )
    coef_set, coef_pull = jax.vjp(coefficients, raw_params)
    gain_now, gain_prev, retain, gain_side = coef_set
    zero_row = jnp.zeros((reach_dev,), jnp.float32)
    unit_row = jnp.ones((reach_dev,), jnp.float32)
    affine_identity = stack_affine((unit_row, zero_row))
    retention = jnp.broadcast_to(retain, (steps_dev, reach_dev))
    zero_flow = jnp.zeros((steps_dev, reach_dev), jnp.float32)

    def route_level(inflow):
        inflow_in = shifted(inflow[-1], "group", 1)
        inflow_before = jnp.concatenate([inflow_in[None], inflow[:-1]], axis=0)
        drive = gain_now * inflow + gain_prev * inflow_before + gain_side * lateral
        powers, local_flow = lax.associative_scan(affine_join, (retention, drive), axis=0)
        edge_scan = carried_in(
            stack_affine((powers[-1], local_flow[-1])),
            "group",
            stacked_affine,
            affine_identity,
            False,
        )
        state_in = edge_scan[1]
        result = local_flow + powers * state_in
        return (result * live_mask, state_in, inflow_in)

    inflow = zero_flow
    outflow, state_in, inflow_in = route_level(inflow)
    for level_step in range(levels - 1):
        upper_flow = shifted(outflow, "level", 1)
        side_flow = shifted(upper_flow, "basin", 1)[:, :outlets]
        source = jnp.concatenate([upper_flow, side_flow], axis=1)
        summed_flow = jnp.zeros((source.shape[0], feeder_count.shape[0]), jnp.float32)
        for sum_upslot in range(up_count):
            picked_flow = jnp.take(source, feeders[sum_upslot], axis=1)
            summed_flow = summed_flow + jnp.where(sum_upslot < feeder_count, picked_flow, 0.0)
        inflow = summed_flow
        outflow, state_in, inflow_in = route_level(inflow)
    adjoint_down = zero_flow
    adjoint = zero_flow
    for level_step in range(levels):
        adjoint_load = live_mask * (cotangent + adjoint_down)
        rev_power, local_adj = lax.associative_scan(
            affine_join, (retention, adjoint_load), axis=0, reverse=True
        )
        edge_adj = carried_in(
            stack_affine((rev_power[0], local_adj[0])),
            "group",
            stacked_affine,
            affine_identity,
            True,
        )
        adjoint_in = edge_adj[1]
        adjoint = local_adj + rev_power * adjoint_in
        if level_step + 1 < levels:
            later_adj = jnp.concatenate([adjoint[1:], adjoint_in[None]], axis=0)
            to_inflow = gain_now * adjoint + gain_prev * later_adj
            spread = jnp.zeros((to_inflow.shape[0], reach_dev + outlets), jnp.float32)
            for upslot in range(up_count):
                spread = spread.at[:, feeders[upslot]].add(
                    jnp.where(upslot < feeder_count, to_inflow, 0.0)
                )
            own_part = spread[:, :reach_dev]
            side_part = spread[:, reach_dev:]
            padded_side = jnp.concatenate(
                [side_part, jnp.zeros((steps_dev, reach_dev - outlets), jnp.float32)], axis=1
            )
            returned = shifted(padded_side, "basin", -1)[:, :outlets]
            combined = own_part.at[:, :outlets].add(returned)
            adjoint_down = shifted(combined, "level", -1)
    flow_before = jnp.concatenate([state_in[None], outflow[:-1]], axis=0)
    inflow_before = jnp.concatenate([inflow_in[None], inflow[:-1]], axis=0)
    coef_grads = (
        jnp.sum(adjoint * inflow, axis=0),
        jnp.sum(adjoint * inflow_before, axis=0),
        jnp.sum(adjoint * flow_before, axis=0),
        jnp.sum(adjoint * lateral, axis=0),
    )
    raw_grad = coef_pull(coef_grads)[0]
    owned_rows = regions // lax.axis_size("basin")
    owner_table = (
        region[None, :]
        == lax.broadcasted_iota(jnp.int32, (owned_rows * lax.axis_size("basin"), reach_dev), 0)
    ).astype(jnp.float32)
    weighted = (owner_table[:, None, :] * raw_grad[None, :, :]).reshape(
        owned_rows * lax.axis_size("basin") * param_count, reach_dev
    )
    summed = jnp.dot(
        weighted, attributes.T, precision=lax.Precision.HIGHEST, preferred_element_type=jnp.float32
    )
    owned_share = lax.psum_scatter(
        jnp.transpose(
            summed.reshape(owned_rows * lax.axis_size("basin"), param_count, attr_count), (0, 2, 1)
        ),
        "basin",
        scatter_dimension=0,
        tiled=True,
    )
    grad_net = lax.psum(owned_share, ("level", "group"))
    return (outflow, grad_net)


def solution(mesh):
    in_specs = (
        P("group", ("level", "basin")),
        P("group", ("level", "basin")),
        P(None, ("level", "basin")),
        P(("level", "basin")),
        P(None, ("level", "basin")),
        P(("level", "basin")),
        P(("level", "basin")),
        P(),
    )
    out_specs = (P("group", ("level", "basin")), P("basin", None, None))
    return jax.shard_map(body, mesh=mesh, in_specs=in_specs, out_specs=out_specs, check_vma=False)
```

profile of v0, /device:TPU:1, one launch (start us, length us, event | category | flops | bytes accessed | tf_op | source)
XLA Modules:
  0.0 403.4 jit_solution(1794903104377895171)
XLA Ops:
  8.6 4.7 %all-gather.12 = f32[2,2,1024]{2,1,0:T(2,128)S(1)} all-gather(f32[1,2,1024]{2,1,0:T(2,128)S(1)} %fusion.55), channel_id=6, replica_groups=mesh['level'=4,'basin'=32,'group'=2] {'group'}, dimensions={0}, use_global_device_ids=true | all-gather | bytes 24576 | tf_op jit(solution)/shard_map/all_gather | solution.py:17
  17.0 6.6 %scatter_custom_fusion = f32[48,1152]{0,1:T(8,128)S(1)} fusion(s32[1024]{0:T(1024)S(1)} %bitcast.231, f32[1024,48]{1,0:T(8,128)} %copy.444, f32[]{:T(128)} %constant.167.clone.1), kind=kCustom, calls=%fused_computation.27 | custom fusion | flops 49152 | bytes 221696 | tf_op jit(solution)/shard_map/scatter-add | solution.py:139
  23.6 6.3 %scatter_fusion = f32[48,1152]{0,1:T(8,128)S(1)} fusion(f32[48,1152]{0,1:T(8,128)S(1)} %scatter_custom_fusion, s32[1024]{0:T(1024)S(1)} %bitcast.203, f32[1024,48]{1,0:T(8,128)S(1)} %copy.445), kind=kCustom, calls=%fused_computation.7 | custom fusion | flops 49152 | bytes 593920 | tf_op jit(solution)/shard_map/scatter-add | solution.py:139
  40.0 5.8 %collective-permute-done.11 = f32[48,1024]{1,0:T(8,128)S(1)} collective-permute-done((f32[48,1024]{1,0:T(8,128)S(1)}, f32[48,1024]{1,0:T(8,128)S(1)}, u32[]{:S(2)}, u32[]{:S(2)}) %collective-permute-start.11) | collective-permute-done | bytes 196640 | tf_op jit(solution)/shard_map/ppermute | solution.py:12
  50.0 3.5 all-gather.13
  57.9 6.3 %scatter_custom_fusion.2 = f32[48,1152]{0,1:T(8,128)S(1)} fusion(s32[1024]{0:T(1024)} %bitcast.232, f32[1024,48]{1,0:T(8,128)S(1)} %copy.449, f32[]{:T(128)} %constant.167.clone.1), kind=kCustom, calls=%fused_computation.25 | custom fusion | flops 49152 | bytes 221696 | tf_op jit(solution)/shard_map/scatter-add | solution.py:139
  64.4 6.4 %scatter_fusion.1 = f32[48,1152]{0,1:T(8,128)S(1)} fusion(f32[48,1152]{0,1:T(8,128)S(1)} %scatter_custom_fusion.2, s32[1024]{0:T(1024)S(1)} %bitcast.204, f32[1024,48]{1,0:T(8,128)S(1)} %copy.450), kind=kCustom, calls=%fused_computation.9 | custom fusion | flops 49152 | bytes 593920 | tf_op jit(solution)/shard_map/scatter-add | solution.py:139
  81.4 4.1 %collective-permute-done.12 = f32[48,1024]{1,0:T(8,128)S(1)} collective-permute-done((f32[48,1024]{1,0:T(8,128)S(1)}, f32[48,1024]{1,0:T(8,128)S(1)}, u32[]{:S(2)}, u32[]{:S(2)}) %collective-permute-start.12) | collective-permute-done | bytes 196640 | tf_op jit(solution)/shard_map/ppermute | solution.py:12
  87.5 5.8 %collective-permute-done.13 = f32[48,1024]{1,0:T(8,128)S(1)} collective-permute-done((f32[48,1024]{1,0:T(8,128)S(1)}, f32[48,1024]{1,0:T(8,128)S(1)}, u32[]{:S(2)}, u32[]{:S(2)}) %collective-permute-start.13) | collective-permute-done | bytes 196640 | tf_op jit(solution)/shard_map/ppermute | solution.py:12
  97.5 3.5 all-gather.14
  104.7 3.9 collective-permute-done.1
  108.5 3.5 collective-permute-start.2
  130.6 6.6 %scatter_custom_fusion.4 = f32[48,1152]{0,1:T(8,128)S(1)} fusion(s32[1024]{0:T(1024)} %bitcast.233, f32[1024,48]{1,0:T(8,128)} %copy.454, f32[]{:T(128)} %constant.167.clone.1), kind=kCustom, calls=%fused_computation.23 | custom fusion | flops 49152 | bytes 221696 | tf_op jit(solution)/shard_map/scatter-add | solution.py:139
  137.9 6.3 %scatter_fusion.2 = f32[48,1152]{0,1:T(8,128)S(1)} fusion(f32[48,1152]{0,1:T(8,128)S(1)} %scatter_custom_fusion.4, s32[1024]{0:T(1024)S(1)} %bitcast.205, f32[1024,48]{1,0:T(8,128)S(1)} %copy.455), kind=kCustom, calls=%fused_computation.11 | custom fusion | flops 49152 | bytes 593920 | tf_op jit(solution)/shard_map/scatter-add | solution.py:139
  153.9 6.8 %collective-permute-done.14 = f32[48,1024]{1,0:T(8,128)S(1)} collective-permute-done((f32[48,1024]{1,0:T(8,128)S(1)}, f32[48,1024]{1,0:T(8,128)S(1)}, u32[]{:S(2)}, u32[]{:S(2)}) %collective-permute-start.14) | collective-permute-done | bytes 196640 | tf_op jit(solution)/shard_map/ppermute | solution.py:12
  162.8 7.1 %collective-permute-done.15 = f32[48,1024]{1,0:T(8,128)S(1)} collective-permute-done((f32[48,1024]{1,0:T(8,128)S(1)}, f32[48,1024]{1,0:T(8,128)S(1)}, u32[]{:S(2)}, u32[]{:S(2)}) %collective-permute-start.15) | collective-permute-done | bytes 196640 | tf_op jit(solution)/shard_map/ppermute | solution.py:12
  178.3 3.4 collective-permute-start.4
  181.6 3.9 collective-permute-done.4
  185.5 4.3 %collective-permute-start.5 = (f32[48,1024]{1,0:T(8,128)S(1)}, f32[48,1024]{1,0:T(8,128)S(1)}, u32[]{:S(2)}, u32[]{:S(2)}) collective-permute-start(f32[48,1024]{1,0:T(8,128)S(1)} %collective-permute-done.4), channel_id=1, source_target_pairs={{0,2},{2,4},{4,6},{6,8},{8,10},{10,12},{12,14},{14,16},{16,18},{18... | collective-permute-start | bytes 589832 | tf_op jit(solution)/shard_map/ppermute | solution.py:12
  210.9 4.1 %collective-permute-start.7 = (f32[48,1024]{1,0:T(8,128)S(1)}, f32[48,1024]{1,0:T(8,128)S(1)}, u32[]{:S(2)}, u32[]{:S(2)}) collective-permute-start(f32[48,1024]{1,0:T(8,128)S(1)} %add_multiply_fusion.4), channel_id=1, source_target_pairs={{0,64},{64,128},{128,192},{1,65},{65,129},{129,193},{2,66},{66,130... | collective-permute-start | bytes 589832 | tf_op jit(solution)/shard_map/ppermute | solution.py:12
  215.1 4.1 %collective-permute-done.7 = f32[48,1024]{1,0:T(8,128)S(1)} collective-permute-done((f32[48,1024]{1,0:T(8,128)S(1)}, f32[48,1024]{1,0:T(8,128)S(1)}, u32[]{:S(2)}, u32[]{:S(2)}) %collective-permute-start.7) | collective-permute-done | bytes 196640 | tf_op jit(solution)/shard_map/ppermute | solution.py:12
  219.1 4.1 %collective-permute-start.8 = (f32[48,1024]{1,0:T(8,128)S(1)}, f32[48,1024]{1,0:T(8,128)S(1)}, u32[]{:S(2)}, u32[]{:S(2)}) collective-permute-start(f32[48,1024]{1,0:T(8,128)S(1)} %collective-permute-done.7), channel_id=1, source_target_pairs={{0,2},{2,4},{4,6},{6,8},{8,10},{10,12},{12,14},{14,16},{16,18},{18... | collective-permute-start | bytes 589832 | tf_op jit(solution)/shard_map/ppermute | solution.py:12
  247.3 115.1 %all-reduce.106 = f32[128,16,2]{1,2,0:T(2,128)S(1)} all-reduce(f32[128,16,2]{1,2,0:T(2,128)S(1)} %copy.459), channel_id=10, replica_groups=mesh['level'=4,'basin'=32,'group'=2] {'basin'}, use_global_device_ids=true, to_apply=%region_11.13.clone | all-reduce | flops 4096 | bytes 32768
  362.3 41.1 %psum.7 = f32[4,16,2]{1,2,0:T(2,128)} all-reduce(f32[4,16,2]{1,2,0:T(2,128)S(1)} %constant_dynamic-slice_fusion), channel_id=1, replica_groups=mesh['level'=4,'basin'=32,'group'=2] {'level','group'}, use_global_device_ids=true, to_apply=%region_12.14 | all-reduce | flops 128 | bytes 1024 | tf_op jit(solution)/shard_map/psum | solution.py:178
  (768 shorter events, 130.3 us)
Async XLA Ops:
  14.8 49.6 %copy-start.46 = (s32[1024,1]{0,1:T(1,128)}, s32[1024,1]{0,1:T(1,128)S(1)}, u32[]{:S(2)}) copy-start(s32[1024,1]{0,1:T(1,128)S(1)} %get-tuple-element.244) | copy-start | bytes 12292
  30.0 8.0 %collective-permute-start.10 = (f32[48,1024]{1,0:T(8,128)S(1)}, f32[48,1024]{1,0:T(8,128)S(1)}, u32[]{:S(2)}, u32[]{:S(2)}) collective-permute-start(f32[48,1024]{1,0:T(8,128)S(1)} %concatenate.272), channel_id=1, source_target_pairs={{2,0},{4,2},{6,4},{8,6},{10,8},{12,10},{14,12},{16,14},{18,16},{20... | collective-permute-start | bytes 589832 | tf_op jit(solution)/shard_map/ppermute | solution.py:12
  31.9 22.0 %collective-permute-start = (f32[1024]{0:T(1024)}, f32[1024]{0:T(1024)}, u32[]{:S(2)}, u32[]{:S(2)}) collective-permute-start(f32[1024]{0:T(1024)} %broadcast_in_dim.52), channel_id=1, source_target_pairs={{0,1},{2,3},{4,5},{6,7},{8,9},{10,11},{12,13},{14,15},{16,17},{18,... | collective-permute-start | bytes 12296 | tf_op jit(solution)/shard_map/ppermute | solution.py:12
  34.0 11.8 %copy-start.2 = (f32[48,1024]{1,0:T(8,128)S(1)}, f32[48,1024]{1,0:T(8,128)}, u32[]{:S(2)}) copy-start(f32[48,1024]{1,0:T(8,128)} %param.17) | copy-start | bytes 589828
  38.7 7.1 %collective-permute-start.11 = (f32[48,1024]{1,0:T(8,128)S(1)}, f32[48,1024]{1,0:T(8,128)S(1)}, u32[]{:S(2)}, u32[]{:S(2)}) collective-permute-start(f32[48,1024]{1,0:T(8,128)S(1)} %fusion.51), channel_id=1, source_target_pairs={{64,0},{128,64},{192,128},{65,1},{129,65},{193,129},{66,2},{130,66... | collective-permute-start | bytes 589832 | tf_op jit(solution)/shard_map/ppermute | solution.py:12
  77.6 8.0 %collective-permute-start.12 = (f32[48,1024]{1,0:T(8,128)S(1)}, f32[48,1024]{1,0:T(8,128)S(1)}, u32[]{:S(2)}, u32[]{:S(2)}) collective-permute-start(f32[48,1024]{1,0:T(8,128)S(1)} %concatenate.279), channel_id=1, source_target_pairs={{2,0},{4,2},{6,4},{8,6},{10,8},{12,10},{14,12},{16,14},{18,16},{20... | collective-permute-start | bytes 589832 | tf_op jit(solution)/shard_map/ppermute | solution.py:12
  86.2 7.1 %collective-permute-start.13 = (f32[48,1024]{1,0:T(8,128)S(1)}, f32[48,1024]{1,0:T(8,128)S(1)}, u32[]{:S(2)}, u32[]{:S(2)}) collective-permute-start(f32[48,1024]{1,0:T(8,128)S(1)} %fusion.52), channel_id=1, source_target_pairs={{64,0},{128,64},{192,128},{65,1},{129,65},{193,129},{66,2},{130,66... | collective-permute-start | bytes 589832 | tf_op jit(solution)/shard_map/ppermute | solution.py:12
  102.4 9.6 %copy-start.61 = (s32[1,1024]{1,0:T(1,128)S(1)}, s32[1,1024]{1,0:T(1,128)}, u32[]{:S(2)}) copy-start(s32[1,1024]{1,0:T(1,128)} %copy-done.60) | copy-start | bytes 12292
  102.4 6.1 %collective-permute-start.1 = (f32[48,1024]{1,0:T(8,128)S(1)}, f32[48,1024]{1,0:T(8,128)S(1)}, u32[]{:S(2)}, u32[]{:S(2)}) collective-permute-start(f32[48,1024]{1,0:T(8,128)S(1)} %get-tuple-element.190), channel_id=1, source_target_pairs={{0,64},{64,128},{128,192},{1,65},{65,129},{129,193},{2,66},{66,130... | collective-permute-start | bytes 589832 | tf_op jit(solution)/shard_map/ppermute | solution.py:12
  104.6 10.7 %copy-start.42 = (s32[1024]{0:T(1024)}, s32[1024]{0:T(1024)S(1)}, u32[]{:S(2)}) copy-start(s32[1024]{0:T(1024)S(1)} %fusion.110) | copy-start | bytes 12292
  108.5 6.6 %collective-permute-start.2 = (f32[48,1024]{1,0:T(8,128)S(1)}, f32[48,1024]{1,0:T(8,128)S(1)}, u32[]{:S(2)}, u32[]{:S(2)}) collective-permute-start(f32[48,1024]{1,0:T(8,128)S(1)} %collective-permute-done.1), channel_id=1, source_target_pairs={{0,2},{2,4},{4,6},{6,8},{8,10},{10,12},{12,14},{14,16},{16,18},{18... | collective-permute-start | bytes 589832 | tf_op jit(solution)/shard_map/ppermute | solution.py:12
  112.1 6.3 %copy-start.44 = (s32[1024]{0:T(1024)}, s32[1024]{0:T(1024)S(1)}, u32[]{:S(2)}) copy-start(s32[1024]{0:T(1024)S(1)} %fusion.111) | copy-start | bytes 12292
  122.1 4.0 collective-permute-start.3
  150.7 9.9 %collective-permute-start.14 = (f32[48,1024]{1,0:T(8,128)S(1)}, f32[48,1024]{1,0:T(8,128)S(1)}, u32[]{:S(2)}, u32[]{:S(2)}) collective-permute-start(f32[48,1024]{1,0:T(8,128)S(1)} %concatenate.286), channel_id=1, source_target_pairs={{2,0},{4,2},{6,4},{8,6},{10,8},{12,10},{14,12},{16,14},{18,16},{20... | collective-permute-start | bytes 589832 | tf_op jit(solution)/shard_map/ppermute | solution.py:12
  161.3 8.6 %collective-permute-start.15 = (f32[48,1024]{1,0:T(8,128)S(1)}, f32[48,1024]{1,0:T(8,128)S(1)}, u32[]{:S(2)}, u32[]{:S(2)}) collective-permute-start(f32[48,1024]{1,0:T(8,128)S(1)} %fusion.53), channel_id=1, source_target_pairs={{64,0},{128,64},{192,128},{65,1},{129,65},{193,129},{66,2},{130,66... | collective-permute-start | bytes 589832 | tf_op jit(solution)/shard_map/ppermute | solution.py:12
  174.1 4.2 %copy-start.12 = (f32[48,1024]{1,0:T(8,128)}, f32[48,1024]{1,0:T(8,128)S(1)}, u32[]{:S(2)}) copy-start(f32[48,1024]{1,0:T(8,128)S(1)} %pad.484) | copy-start | bytes 589828
  178.3 7.3 %collective-permute-start.4 = (f32[48,1024]{1,0:T(8,128)S(1)}, f32[48,1024]{1,0:T(8,128)S(1)}, u32[]{:S(2)}, u32[]{:S(2)}) collective-permute-start(f32[48,1024]{1,0:T(8,128)S(1)} %add_multiply_fusion.5), channel_id=1, source_target_pairs={{0,64},{64,128},{128,192},{1,65},{65,129},{129,193},{2,66},{66,130... | collective-permute-start | bytes 589832 | tf_op jit(solution)/shard_map/ppermute | solution.py:12
  185.5 7.3 %collective-permute-start.5 = (f32[48,1024]{1,0:T(8,128)S(1)}, f32[48,1024]{1,0:T(8,128)S(1)}, u32[]{:S(2)}, u32[]{:S(2)}) collective-permute-start(f32[48,1024]{1,0:T(8,128)S(1)} %collective-permute-done.4), channel_id=1, source_target_pairs={{0,2},{2,4},{4,6},{6,8},{8,10},{10,12},{12,14},{14,16},{16,18},{18... | collective-permute-start | bytes 589832 | tf_op jit(solution)/shard_map/ppermute | solution.py:12
  193.5 2.8 copy-start.45
  200.1 4.0 collective-permute-start.6
  210.9 8.2 %collective-permute-start.7 = (f32[48,1024]{1,0:T(8,128)S(1)}, f32[48,1024]{1,0:T(8,128)S(1)}, u32[]{:S(2)}, u32[]{:S(2)}) collective-permute-start(f32[48,1024]{1,0:T(8,128)S(1)} %add_multiply_fusion.4), channel_id=1, source_target_pairs={{0,64},{64,128},{128,192},{1,65},{65,129},{129,193},{2,66},{66,130... | collective-permute-start | bytes 589832 | tf_op jit(solution)/shard_map/ppermute | solution.py:12
  219.1 7.3 %collective-permute-start.8 = (f32[48,1024]{1,0:T(8,128)S(1)}, f32[48,1024]{1,0:T(8,128)S(1)}, u32[]{:S(2)}, u32[]{:S(2)}) collective-permute-start(f32[48,1024]{1,0:T(8,128)S(1)} %collective-permute-done.7), channel_id=1, source_target_pairs={{0,2},{2,4},{4,6},{6,8},{8,10},{10,12},{12,14},{14,16},{16,18},{18... | collective-permute-start | bytes 589832 | tf_op jit(solution)/shard_map/ppermute | solution.py:12
  233.2 3.4 copy-start.13
  233.3 3.9 collective-permute-start.9
  (99 other events, 81.4 us)
where the time goes:
time: 406 us; the launch traced here: 403 us
  blocking collectives  179 us (44%)
  local copies, waits for them, and re-layouts  72.7 us (18%)
  waiting for transfers between devices  59 us (15%)
  other arithmetic  49.8 us (12%)
  starting transfers between devices  34.8 us (9%)
  between operations  5.91 us (1%)
    unnamed x1, blocking collectives  115 us
    ppermute x16, waiting for transfers between devices, shifted(): lax.ppermute(value, axis, [(source, source + steps) for source in range(l...  59 us
    psum x1, blocking collectives, body(): grad_net = lax.psum(owned_share, ('level', 'group'))  41.1 us
    scatter-add x6, other arithmetic, body(): spread.at[:, feeders[upslot]]  38.4 us
    ppermute x16, starting transfers between devices, shifted(): lax.ppermute(value, axis, [(source, source + steps) for source in range(l...  34.8 us
    all_gather x8, blocking collectives, carried_in(): pieces = lax.all_gather(value, axis)  23 us
    unnamed x179, local copies, waits for them, and re-layouts  23 us
    gather x12, local copies, waits for them, and re-layouts, body(): picked_flow = jnp.take(source, feeders[sum_upslot], axis=1)  17.9 us
  transfers between devices with their start and end apart: 16, of which 15 were waited for; matrix products, arithmetic and copies ran while one was open for 1% of the time, Pallas kernels for 0%

commit v1 on v0

--- a/solution.py
+++ b/solution.py
@@ -10,6 +10,41 @@
     count = lax.axis_size(axis)
     leading, last = (max(0, -steps), min(count, count - steps))
     return lax.ppermute(value, axis, [(source, source + steps) for source in range(leading, last)])
+
+
+def diagonal(value, steps):
+    levels, basins = lax.axis_size("level"), lax.axis_size("basin")
+    pairs = []
+    for level in range(max(0, -steps), min(levels, levels - steps)):
+        for basin in range(max(0, -steps), min(basins, basins - steps)):
+            pairs.append((level * basins + basin, (level + steps) * basins + basin + steps))
+    return lax.ppermute(value, ("level", "basin"), pairs)
+
+
+def exchanged(value, axis, mask):
+    count = lax.axis_size(axis)
+    return lax.ppermute(value, axis, [(source, source ^ mask) for source in range(count)])
+
+
+def scattered_sum(blocks, axis):
+    count, mine = (lax.axis_size(axis), lax.axis_index(axis))
+    width = count
+    while width > 1:
+        width //= 2
+        lower, upper = blocks[:width], blocks[width:]
+        high = (mine & width) > 0
+        kept = jnp.where(high, upper, lower)
+        sent = jnp.where(high, lower, upper)
+        blocks = kept + exchanged(sent, axis, width)
+    return blocks[0]
+
+
+def butterfly_sum(value, axis):
+    mask = 1
+    while mask < lax.axis_size(axis):
+        value = value + exchanged(value, axis, mask)
+        mask *= 2
+    return value
 
 
 def carried_in(value, axis, join, neutral, backward):
@@ -107,7 +142,7 @@
     outflow, state_in, inflow_in = route_level(inflow)
     for level_step in range(levels - 1):
         upper_flow = shifted(outflow, "level", 1)
-        side_flow = shifted(upper_flow, "basin", 1)[:, :outlets]
+        side_flow = diagonal(outflow[:, :outlets], 1)
         source = jnp.concatenate([upper_flow, side_flow], axis=1)
         summed_flow = jnp.zeros((source.shape[0], feeder_count.shape[0]), jnp.float32)
         for sum_upslot in range(up_count):
@@ -141,12 +176,8 @@
                 )
             own_part = spread[:, :reach_dev]
             side_part = spread[:, reach_dev:]
-            padded_side = jnp.concatenate(
-                [side_part, jnp.zeros((steps_dev, reach_dev - outlets), jnp.float32)], axis=1
-            )
-            returned = shifted(padded_side, "basin", -1)[:, :outlets]
-            combined = own_part.at[:, :outlets].add(returned)
-            adjoint_down = shifted(combined, "level", -1)
+            returned = diagonal(side_part, -1)
+            adjoint_down = shifted(own_part, "level", -1).at[:, :outlets].add(returned)
     flow_before = jnp.concatenate([state_in[None], outflow[:-1]], axis=0)
     inflow_before = jnp.concatenate([inflow_in[None], inflow[:-1]], axis=0)
     coef_grads = (
@@ -158,24 +189,20 @@
     raw_grad = coef_pull(coef_grads)[0]
     owned_rows = regions // lax.axis_size("basin")
     owner_table = (
-        region[None, :]
-        == lax.broadcasted_iota(jnp.int32, (owned_rows * lax.axis_size("basin"), reach_dev), 0)
+        region[None, :] == lax.broadcasted_iota(jnp.int32, (regions, reach_dev), 0)
     ).astype(jnp.float32)
     weighted = (owner_table[:, None, :] * raw_grad[None, :, :]).reshape(
-        owned_rows * lax.axis_size("basin") * param_count, reach_dev
+        regions * param_count, reach_dev
     )
     summed = jnp.dot(
         weighted, attributes.T, precision=lax.Precision.HIGHEST, preferred_element_type=jnp.float32
     )
-    owned_share = lax.psum_scatter(
-        jnp.transpose(
-            summed.reshape(owned_rows * lax.axis_size("basin"), param_count, attr_count), (0, 2, 1)
-        ),
-        "basin",
-        scatter_dimension=0,
-        tiled=True,
-    )
-    grad_net = lax.psum(owned_share, ("level", "group"))
+    local_grad = jnp.transpose(summed.reshape(regions, param_count, attr_count), (0, 2, 1))
+    basins = lax.axis_size("basin")
+    owned_share = scattered_sum(
+        local_grad.reshape(basins, owned_rows, attr_count, param_count), "basin"
+    )
+    grad_net = butterfly_sum(butterfly_sum(owned_share, "group"), "level")
     return (outflow, grad_net)
 
 

time: 406 us -> 250 us (0.62)
  blocking collectives: 179 us -> 19.8 us
  starting transfers between devices: 34.8 us -> 58.2 us
  waiting for transfers between devices: 59 us -> 39.4 us
    unnamed x1 -> x0, blocking collectives: 115 us -> none
    ppermute x16 -> x10, waiting for transfers between devices: 59 us -> 10.1 us  [shifted(): lax.ppermute(value, axis, [(source, source + steps) for source in range(l...]
    psum x1 -> x0, blocking collectives: 41.1 us -> none  [body(): grad_net = lax.psum(owned_share, ('level', 'group'))]
    ppermute x0 -> x14, starting transfers between devices: none -> 39.8 us  [the longest x8 24.1 us: exchanged(): lax.ppermute(value, axis, [(source, source ^ mask) for source in range(co...]
    ppermute x0 -> x14, waiting for transfers between devices: none -> 29.3 us  [the longest x8 20.5 us: exchanged(): lax.ppermute(value, axis, [(source, source ^ mask) for source in range(co...]
    ppermute x16 -> x10, starting transfers between devices: 34.8 us -> 18.4 us  [shifted(): lax.ppermute(value, axis, [(source, source + steps) for source in range(l...]
    unnamed x179 -> x165, local copies, waits for them, and re-layouts: 23 us -> 20.7 us
  transfers between devices with their start and end apart: 16 -> 24, of which waited for: 15 -> 20; matrix products, arithmetic and copies ran while one was open for 1% -> 2% of each run, Pallas kernels for 0% -> 0%
where the time goes in v1:
time: 250 us; the launch traced here: 246 us
  local copies, waits for them, and re-layouts  70.5 us (28%)
  starting transfers between devices  58.2 us (23%)
  other arithmetic  50.5 us (20%)
  waiting for transfers between devices  39.4 us (16%)
  blocking collectives  19.8 us (8%)
  between operations  5.3 us (2%)
    scatter-add x6, other arithmetic, body(): spread.at[:, feeders[upslot]]  38.4 us
    ppermute x8, starting transfers between devices, exchanged(): lax.ppermute(value, axis, [(source, source ^ mask) for source in range(co...  24.1 us
    unnamed x165, local copies, waits for them, and re-layouts  20.7 us
    ppermute x8, waiting for transfers between devices, exchanged(): lax.ppermute(value, axis, [(source, source ^ mask) for source in range(co...  20.5 us
    all_gather x8, blocking collectives, carried_in(): pieces = lax.all_gather(value, axis)  19.8 us
    ppermute x10, starting transfers between devices, shifted(): lax.ppermute(value, axis, [(source, source + steps) for source in range(l...  18.4 us
    gather x12, local copies, waits for them, and re-layouts, body(): picked_flow = jnp.take(source, feeders[sum_upslot], axis=1)  17.9 us
    ppermute x6, starting transfers between devices, diagonal(): return lax.ppermute(value, ('level', 'basin'), pairs)  15.7 us
  transfers between devices with their start and end apart: 24, of which 20 were waited for; matrix products, arithmetic and copies ran while one was open for 2% of the time, Pallas kernels for 0%

profile of v1, /device:TPU:1, one launch (start us, length us, event | category | flops | bytes accessed | tf_op | source)
XLA Modules:
  0.0 245.7 jit_solution(8620275619128763942)
XLA Ops:
  8.6 4.7 %all-gather.12 = f32[2,2,1024]{2,1,0:T(2,128)S(1)} all-gather(f32[1,2,1024]{2,1,0:T(2,128)S(1)} %fusion.55), channel_id=6, replica_groups=mesh['level'=4,'basin'=32,'group'=2] {'group'}, dimensions={0}, use_global_device_ids=true | all-gather | bytes 24576 | tf_op jit(solution)/shard_map/all_gather | solution.py:52
  17.0 6.6 %scatter_custom_fusion = f32[48,1152]{0,1:T(8,128)S(1)} fusion(s32[1024]{0:T(1024)S(1)} %bitcast.237, f32[1024,48]{1,0:T(8,128)} %copy.452, f32[]{:T(128)} %constant.173.clone.1), kind=kCustom, calls=%fused_computation.27 | custom fusion | flops 49152 | bytes 221696 | tf_op jit(solution)/shard_map/scatter-add | solution.py:174
  23.6 6.3 %scatter_fusion = f32[48,1152]{0,1:T(8,128)S(1)} fusion(f32[48,1152]{0,1:T(8,128)S(1)} %scatter_custom_fusion, s32[1024]{0:T(1024)S(1)} %bitcast.207, f32[1024,48]{1,0:T(8,128)S(1)} %copy.453), kind=kCustom, calls=%fused_computation.7 | custom fusion | flops 49152 | bytes 593920 | tf_op jit(solution)/shard_map/scatter-add | solution.py:174
  50.0 6.3 %scatter_custom_fusion.2 = f32[48,1152]{0,1:T(8,128)S(1)} fusion(s32[1024]{0:T(1024)} %bitcast.238, f32[1024,48]{1,0:T(8,128)S(1)} %copy.456, f32[]{:T(128)} %constant.173.clone.1), kind=kCustom, calls=%fused_computation.25 | custom fusion | flops 49152 | bytes 221696 | tf_op jit(solution)/shard_map/scatter-add | solution.py:174
  56.5 6.4 %scatter_fusion.1 = f32[48,1152]{0,1:T(8,128)S(1)} fusion(f32[48,1152]{0,1:T(8,128)S(1)} %scatter_custom_fusion.2, s32[1024]{0:T(1024)S(1)} %bitcast.208, f32[1024,48]{1,0:T(8,128)S(1)} %copy.457), kind=kCustom, calls=%fused_computation.9 | custom fusion | flops 49152 | bytes 593920 | tf_op jit(solution)/shard_map/scatter-add | solution.py:174
  87.5 2.9 %collective-permute-start.1 = (f32[48,1024]{1,0:T(8,128)}, f32[48,1024]{1,0:T(8,128)S(1)}, u32[]{:S(2)}, u32[]{:S(2)}) collective-permute-start(f32[48,1024]{1,0:T(8,128)} %get-tuple-element.192), channel_id=1, source_target_pairs={{0,64},{64,128},{128,192},{1,65},{65,129},{129,193},{2,66},{66,130... | collective-permute-start | bytes 589832 | tf_op jit(solution)/shard_map/ppermute | solution.py:12
  90.4 3.3 %collective-permute-start.2 = (f32[48,128]{1,0:T(8,128)S(1)}, f32[48,128]{1,0:T(8,128)S(1)}, u32[]{:S(2)}, u32[]{:S(2)}) collective-permute-start(f32[48,128]{1,0:T(8,128)S(1)} %slice.1614), channel_id=1, source_target_pairs={{0,66},{2,68},{4,70},{6,72},{8,74},{10,76},{12,78},{14,80},{16,82}... | collective-permute-start | bytes 73736 | tf_op jit(solution)/shard_map/ppermute | solution.py:21
  95.3 2.8 %gather_fusion.1 = f32[1024,48]{1,0:T(8,128)S(1)} fusion(f32[48,1152]{0,1:T(8,128)S(1)} %copy.440, s32[1024]{0:T(1024)S(1)} %copy-done.40), kind=kCustom, calls=%fused_computation.1.clone | custom fusion | bytes 397312 | tf_op jit(solution)/shard_map/jit(_take)/gather | solution.py:149
  98.3 2.8 %gather_fusion = f32[1024,48]{1,0:T(8,128)S(1)} fusion(f32[48,1152]{0,1:T(8,128)S(1)} %copy.440, s32[1024]{0:T(1024)S(1)} %fusion.111), kind=kCustom, calls=%fused_computation.clone | custom fusion | bytes 397312 | tf_op jit(solution)/shard_map/jit(_take)/gather | solution.py:149
  110.1 6.6 %scatter_custom_fusion.4 = f32[48,1152]{0,1:T(8,128)S(1)} fusion(s32[1024]{0:T(1024)} %bitcast.239, f32[1024,48]{1,0:T(8,128)} %copy.460, f32[]{:T(128)} %constant.173.clone.1), kind=kCustom, calls=%fused_computation.23 | custom fusion | flops 49152 | bytes 221696 | tf_op jit(solution)/shard_map/scatter-add | solution.py:174
  117.3 6.3 %scatter_fusion.2 = f32[48,1152]{0,1:T(8,128)S(1)} fusion(f32[48,1152]{0,1:T(8,128)S(1)} %scatter_custom_fusion.4, s32[1024]{0:T(1024)S(1)} %bitcast.209, f32[1024,48]{1,0:T(8,128)S(1)} %copy.461), kind=kCustom, calls=%fused_computation.11 | custom fusion | flops 49152 | bytes 593920 | tf_op jit(solution)/shard_map/scatter-add | solution.py:174
  133.8 3.6 %collective-permute-done.15 = f32[48,128]{1,0:T(8,128)S(1)} collective-permute-done((f32[48,128]{1,0:T(8,128)S(1)}, f32[48,128]{1,0:T(8,128)S(1)}, u32[]{:S(2)}, u32[]{:S(2)}) %collective-permute-start.15) | collective-permute-done | bytes 24608 | tf_op jit(solution)/shard_map/ppermute | solution.py:21
  147.1 3.4 %collective-permute-start.4 = (f32[48,1024]{1,0:T(8,128)S(1)}, f32[48,1024]{1,0:T(8,128)S(1)}, u32[]{:S(2)}, u32[]{:S(2)}) collective-permute-start(f32[48,1024]{1,0:T(8,128)S(1)} %add_multiply_fusion.5), channel_id=1, source_target_pairs={{0,64},{64,128},{128,192},{1,65},{65,129},{129,193},{2,66},{66,130... | collective-permute-start | bytes 589832 | tf_op jit(solution)/shard_map/ppermute | solution.py:12
  150.5 3.9 %collective-permute-start.5 = (f32[48,128]{1,0:T(8,128)S(1)}, f32[48,128]{1,0:T(8,128)S(1)}, u32[]{:S(2)}, u32[]{:S(2)}) collective-permute-start(f32[48,128]{1,0:T(8,128)S(1)} %slice.1637), channel_id=1, source_target_pairs={{0,66},{2,68},{4,70},{6,72},{8,74},{10,76},{12,78},{14,80},{16,82}... | collective-permute-start | bytes 73736 | tf_op jit(solution)/shard_map/ppermute | solution.py:21
  158.9 2.8 %gather_fusion.2 = f32[1024,48]{1,0:T(8,128)S(1)} fusion(f32[48,1152]{0,1:T(8,128)S(1)} %copy.444, s32[1024]{0:T(1024)S(1)} %copy-done.43), kind=kCustom, calls=%fused_computation.2.clone | custom fusion | bytes 397312 | tf_op jit(solution)/shard_map/jit(_take)/gather | solution.py:149
  172.9 2.8 %collective-permute-start.7 = (f32[48,1024]{1,0:T(8,128)S(1)}, f32[48,1024]{1,0:T(8,128)S(1)}, u32[]{:S(2)}, u32[]{:S(2)}) collective-permute-start(f32[48,1024]{1,0:T(8,128)S(1)} %add_multiply_fusion.4), channel_id=1, source_target_pairs={{0,64},{64,128},{128,192},{1,65},{65,129},{129,193},{2,66},{66,130... | collective-permute-start | bytes 589832 | tf_op jit(solution)/shard_map/ppermute | solution.py:12
  175.7 4.5 %collective-permute-start.8 = (f32[48,128]{1,0:T(8,128)S(1)}, f32[48,128]{1,0:T(8,128)S(1)}, u32[]{:S(2)}, u32[]{:S(2)}) collective-permute-start(f32[48,128]{1,0:T(8,128)S(1)} %slice.1660), channel_id=1, source_target_pairs={{0,66},{2,68},{4,70},{6,72},{8,74},{10,76},{12,78},{14,80},{16,82}... | collective-permute-start | bytes 73736 | tf_op jit(solution)/shard_map/ppermute | solution.py:21
  181.4 2.8 %gather_fusion.5 = f32[1024,48]{1,0:T(8,128)S(1)} fusion(f32[48,1152]{0,1:T(8,128)S(1)} %copy.448, s32[1024]{0:T(1024)S(1)} %copy-done.41), kind=kCustom, calls=%fused_computation.5.clone | custom fusion | bytes 397312 | tf_op jit(solution)/shard_map/jit(_take)/gather | solution.py:149
  184.2 2.8 %gather_fusion.4 = f32[1024,48]{1,0:T(8,128)S(1)} fusion(f32[48,1152]{0,1:T(8,128)S(1)} %copy.448, s32[1024]{0:T(1024)S(1)} %copy-done.43), kind=kCustom, calls=%fused_computation.4.clone | custom fusion | bytes 397312 | tf_op jit(solution)/shard_map/jit(_take)/gather | solution.py:149
  200.2 11.5 %collective-permute-start.16 = (f32[16,4,16,2]{2,1,0,3:T(4,128)S(1)}, f32[16,4,16,2]{2,1,0,3:T(4,128)S(1)}, u32[]{:S(2)}, u32[]{:S(2)}) collective-permute-start(f32[16,4,16,2]{2,1,0,3:T(4,128)S(1)} %bitcast.210), channel_id=1, source_target_pairs={{0,32},{2,34},{4,36},{6,38},{8,40},{10,42},{12,44},{14,46},{16,48}... | collective-permute-start | bytes 24584 | tf_op jit(solution)/shard_map/ppermute | solution.py:26
  217.1 6.5 %collective-permute-done.18 = f32[4,4,16,2]{2,1,0,3:T(4,128)S(1)} collective-permute-done((f32[4,4,16,2]{2,1,0,3:T(4,128)S(1)}, f32[4,4,16,2]{2,1,0,3:T(4,128)S(1)}, u32[]{:S(2)}, u32[]{:S(2)}) %collective-permute-start.18) | collective-permute-done | bytes 2080 | tf_op jit(solution)/shard_map/ppermute | solution.py:26
  223.7 3.4 %collective-permute-done.19 = f32[2,4,16,2]{2,1,0,3:T(4,128)S(1)} collective-permute-done((f32[2,4,16,2]{2,1,0,3:T(4,128)S(1)}, f32[2,4,16,2]{2,1,0,3:T(4,128)S(1)}, u32[]{:S(2)}, u32[]{:S(2)}) %collective-permute-start.19) | collective-permute-done | bytes 1056 | tf_op jit(solution)/shard_map/ppermute | solution.py:26
  229.7 5.3 %collective-permute-start.21 = (f32[4,16,2]{1,0,2:T(4,128)S(1)}, f32[4,16,2]{1,0,2:T(4,128)S(1)}, u32[]{:S(2)}, u32[]{:S(2)}) collective-permute-start(f32[4,16,2]{1,0,2:T(4,128)S(1)} %add_bitcast_fusion), channel_id=1, source_target_pairs={{0,1},{1,0},{2,3},{3,2},{4,5},{5,4},{6,7},{7,6},{8,9},{9,8},{10,11... | collective-permute-start | bytes 1544 | tf_op jit(solution)/shard_map/ppermute | solution.py:26
  235.8 4.3 %collective-permute-start.22 = (f32[4,16,2]{1,0,2:T(4,128)S(1)}, f32[4,16,2]{1,0,2:T(4,128)S(1)}, u32[]{:S(2)}, u32[]{:S(2)}) collective-permute-start(f32[4,16,2]{1,0,2:T(4,128)S(1)} %add.1242), channel_id=1, source_target_pairs={{0,64},{64,0},{128,192},{192,128},{1,65},{65,1},{129,193},{193,129... | collective-permute-start | bytes 1544 | tf_op jit(solution)/shard_map/ppermute | solution.py:26
  (779 shorter events, 127.9 us)
Async XLA Ops:
  30.1 8.7 %collective-permute-start.10 = (f32[48,1024]{1,0:T(8,128)S(1)}, f32[48,1024]{1,0:T(8,128)S(1)}, u32[]{:S(2)}, u32[]{:S(2)}) collective-permute-start(f32[48,1024]{1,0:T(8,128)S(1)} %copy.473), channel_id=1, source_target_pairs={{64,0},{128,64},{192,128},{65,1},{129,65},{193,129},{66,2},{130,66... | collective-permute-start | bytes 589832 | tf_op jit(solution)/shard_map/ppermute | solution.py:12
  31.6 5.6 %collective-permute-start.11 = (f32[48,128]{1,0:T(8,128)S(1)}, f32[48,128]{1,0:T(8,128)S(1)}, u32[]{:S(2)}, u32[]{:S(2)}) collective-permute-start(f32[48,128]{1,0:T(8,128)S(1)} %copy.474), channel_id=1, source_target_pairs={{66,0},{68,2},{70,4},{72,6},{74,8},{76,10},{78,12},{80,14},{82,16}... | collective-permute-start | bytes 73736 | tf_op jit(solution)/shard_map/ppermute | solution.py:21
  32.9 13.7 %collective-permute-start = (f32[1024]{0:T(1024)S(1)}, f32[1024]{0:T(1024)S(1)}, u32[]{:S(2)}, u32[]{:S(2)}) collective-permute-start(f32[1024]{0:T(1024)S(1)} %broadcast_in_dim.52), channel_id=1, source_target_pairs={{0,1},{2,3},{4,5},{6,7},{8,9},{10,11},{12,13},{14,15},{16,17},{18,... | collective-permute-start | bytes 12296 | tf_op jit(solution)/shard_map/ppermute | solution.py:12
  68.7 8.5 %collective-permute-start.12 = (f32[48,1024]{1,0:T(8,128)S(1)}, f32[48,1024]{1,0:T(8,128)S(1)}, u32[]{:S(2)}, u32[]{:S(2)}) collective-permute-start(f32[48,1024]{1,0:T(8,128)S(1)} %copy.475), channel_id=1, source_target_pairs={{64,0},{128,64},{192,128},{65,1},{129,65},{193,129},{66,2},{130,66... | collective-permute-start | bytes 589832 | tf_op jit(solution)/shard_map/ppermute | solution.py:12
  70.1 5.6 %collective-permute-start.13 = (f32[48,128]{1,0:T(8,128)S(1)}, f32[48,128]{1,0:T(8,128)S(1)}, u32[]{:S(2)}, u32[]{:S(2)}) collective-permute-start(f32[48,128]{1,0:T(8,128)S(1)} %copy.476), channel_id=1, source_target_pairs={{66,0},{68,2},{70,4},{72,6},{74,8},{76,10},{78,12},{80,14},{82,16}... | collective-permute-start | bytes 73736 | tf_op jit(solution)/shard_map/ppermute | solution.py:21
  87.5 7.1 %collective-permute-start.1 = (f32[48,1024]{1,0:T(8,128)}, f32[48,1024]{1,0:T(8,128)S(1)}, u32[]{:S(2)}, u32[]{:S(2)}) collective-permute-start(f32[48,1024]{1,0:T(8,128)} %get-tuple-element.192), channel_id=1, source_target_pairs={{0,64},{64,128},{128,192},{1,65},{65,129},{129,193},{2,66},{66,130... | collective-permute-start | bytes 589832 | tf_op jit(solution)/shard_map/ppermute | solution.py:12
  90.4 4.2 %collective-permute-start.2 = (f32[48,128]{1,0:T(8,128)S(1)}, f32[48,128]{1,0:T(8,128)S(1)}, u32[]{:S(2)}, u32[]{:S(2)}) collective-permute-start(f32[48,128]{1,0:T(8,128)S(1)} %slice.1614), channel_id=1, source_target_pairs={{0,66},{2,68},{4,70},{6,72},{8,74},{10,76},{12,78},{14,80},{16,82}... | collective-permute-start | bytes 73736 | tf_op jit(solution)/shard_map/ppermute | solution.py:21
  102.1 3.4 %collective-permute-start.3 = (f32[1024]{0:T(1024)S(1)}, f32[1024]{0:T(1024)S(1)}, u32[]{:S(2)}, u32[]{:S(2)}) collective-permute-start(f32[1024]{0:T(1024)S(1)} %bitcast.235), channel_id=1, source_target_pairs={{0,1},{2,3},{4,5},{6,7},{8,9},{10,11},{12,13},{14,15},{16,17},{18,... | collective-permute-start | bytes 12296 | tf_op jit(solution)/shard_map/ppermute | solution.py:12
  129.1 9.3 %collective-permute-start.14 = (f32[48,1024]{1,0:T(8,128)S(1)}, f32[48,1024]{1,0:T(8,128)S(1)}, u32[]{:S(2)}, u32[]{:S(2)}) collective-permute-start(f32[48,1024]{1,0:T(8,128)S(1)} %copy.477), channel_id=1, source_target_pairs={{64,0},{128,64},{192,128},{65,1},{129,65},{193,129},{66,2},{130,66... | collective-permute-start | bytes 589832 | tf_op jit(solution)/shard_map/ppermute | solution.py:12
  130.5 6.9 %collective-permute-start.15 = (f32[48,128]{1,0:T(8,128)S(1)}, f32[48,128]{1,0:T(8,128)S(1)}, u32[]{:S(2)}, u32[]{:S(2)}) collective-permute-start(f32[48,128]{1,0:T(8,128)S(1)} %copy.478), channel_id=1, source_target_pairs={{66,0},{68,2},{70,4},{72,6},{74,8},{76,10},{78,12},{80,14},{82,16}... | collective-permute-start | bytes 73736 | tf_op jit(solution)/shard_map/ppermute | solution.py:21
  147.1 8.3 %collective-permute-start.4 = (f32[48,1024]{1,0:T(8,128)S(1)}, f32[48,1024]{1,0:T(8,128)S(1)}, u32[]{:S(2)}, u32[]{:S(2)}) collective-permute-start(f32[48,1024]{1,0:T(8,128)S(1)} %add_multiply_fusion.5), channel_id=1, source_target_pairs={{0,64},{64,128},{128,192},{1,65},{65,129},{129,193},{2,66},{66,130... | collective-permute-start | bytes 589832 | tf_op jit(solution)/shard_map/ppermute | solution.py:12
  150.5 4.9 %collective-permute-start.5 = (f32[48,128]{1,0:T(8,128)S(1)}, f32[48,128]{1,0:T(8,128)S(1)}, u32[]{:S(2)}, u32[]{:S(2)}) collective-permute-start(f32[48,128]{1,0:T(8,128)S(1)} %slice.1637), channel_id=1, source_target_pairs={{0,66},{2,68},{4,70},{6,72},{8,74},{10,76},{12,78},{14,80},{16,82}... | collective-permute-start | bytes 73736 | tf_op jit(solution)/shard_map/ppermute | solution.py:21
  162.6 3.4 %collective-permute-start.6 = (f32[1024]{0:T(1024)S(1)}, f32[1024]{0:T(1024)S(1)}, u32[]{:S(2)}, u32[]{:S(2)}) collective-permute-start(f32[1024]{0:T(1024)S(1)} %bitcast.236), channel_id=1, source_target_pairs={{0,1},{2,3},{4,5},{6,7},{8,9},{10,11},{12,13},{14,15},{16,17},{18,... | collective-permute-start | bytes 12296 | tf_op jit(solution)/shard_map/ppermute | solution.py:12
  172.9 8.3 %collective-permute-start.7 = (f32[48,1024]{1,0:T(8,128)S(1)}, f32[48,1024]{1,0:T(8,128)S(1)}, u32[]{:S(2)}, u32[]{:S(2)}) collective-permute-start(f32[48,1024]{1,0:T(8,128)S(1)} %add_multiply_fusion.4), channel_id=1, source_target_pairs={{0,64},{64,128},{128,192},{1,65},{65,129},{129,193},{2,66},{66,130... | collective-permute-start | bytes 589832 | tf_op jit(solution)/shard_map/ppermute | solution.py:12
  175.7 5.4 %collective-permute-start.8 = (f32[48,128]{1,0:T(8,128)S(1)}, f32[48,128]{1,0:T(8,128)S(1)}, u32[]{:S(2)}, u32[]{:S(2)}) collective-permute-start(f32[48,128]{1,0:T(8,128)S(1)} %slice.1660), channel_id=1, source_target_pairs={{0,66},{2,68},{4,70},{6,72},{8,74},{10,76},{12,78},{14,80},{16,82}... | collective-permute-start | bytes 73736 | tf_op jit(solution)/shard_map/ppermute | solution.py:21
  187.9 3.4 %collective-permute-start.9 = (f32[1024]{0:T(1024)S(1)}, f32[1024]{0:T(1024)S(1)}, u32[]{:S(2)}, u32[]{:S(2)}) collective-permute-start(f32[1024]{0:T(1024)S(1)} %bitcast.234), channel_id=1, source_target_pairs={{0,1},{2,3},{4,5},{6,7},{8,9},{10,11},{12,13},{14,15},{16,17},{18,... | collective-permute-start | bytes 12296 | tf_op jit(solution)/shard_map/ppermute | solution.py:12
  200.2 13.8 %collective-permute-start.16 = (f32[16,4,16,2]{2,1,0,3:T(4,128)S(1)}, f32[16,4,16,2]{2,1,0,3:T(4,128)S(1)}, u32[]{:S(2)}, u32[]{:S(2)}) collective-permute-start(f32[16,4,16,2]{2,1,0,3:T(4,128)S(1)} %bitcast.210), channel_id=1, source_target_pairs={{0,32},{2,34},{4,36},{6,38},{8,40},{10,42},{12,44},{14,46},{16,48}... | collective-permute-start | bytes 24584 | tf_op jit(solution)/shard_map/ppermute | solution.py:26
  214.1 2.9 %collective-permute-start.17 = (f32[8,4,16,2]{2,1,0,3:T(4,128)S(1)}, f32[8,4,16,2]{2,1,0,3:T(4,128)S(1)}, u32[]{:S(2)}, u32[]{:S(2)}) collective-permute-start(f32[8,4,16,2]{2,1,0,3:T(4,128)S(1)} %slice_select_fusion), channel_id=1, source_target_pairs={{0,16},{2,18},{4,20},{6,22},{8,24},{10,26},{12,28},{14,30},{16,0},... | collective-permute-start | bytes 12296 | tf_op jit(solution)/shard_map/ppermute | solution.py:26
  217.0 6.6 %collective-permute-start.18 = (f32[4,4,16,2]{2,1,0,3:T(4,128)S(1)}, f32[4,4,16,2]{2,1,0,3:T(4,128)S(1)}, u32[]{:S(2)}, u32[]{:S(2)}) collective-permute-start(f32[4,4,16,2]{2,1,0,3:T(4,128)S(1)} %slice_select_fusion.3), channel_id=1, source_target_pairs={{0,8},{2,10},{4,12},{6,14},{8,0},{10,2},{12,4},{14,6},{16,24},{18,... | collective-permute-start | bytes 6152 | tf_op jit(solution)/shard_map/ppermute | solution.py:26
  223.6 3.5 %collective-permute-start.19 = (f32[2,4,16,2]{2,1,0,3:T(4,128)S(1)}, f32[2,4,16,2]{2,1,0,3:T(4,128)S(1)}, u32[]{:S(2)}, u32[]{:S(2)}) collective-permute-start(f32[2,4,16,2]{2,1,0,3:T(4,128)S(1)} %slice_select_fusion.4), channel_id=1, source_target_pairs={{0,4},{2,6},{4,0},{6,2},{8,12},{10,14},{12,8},{14,10},{16,20},{18,... | collective-permute-start | bytes 3080 | tf_op jit(solution)/shard_map/ppermute | solution.py:26
  227.1 2.5 %collective-permute-start.20 = (f32[1,4,16,2]{2,1,0,3:T(4,128)S(1)}, f32[1,4,16,2]{2,1,0,3:T(4,128)S(1)}, u32[]{:S(2)}, u32[]{:S(2)}) collective-permute-start(f32[1,4,16,2]{2,1,0,3:T(4,128)S(1)} %slice_select_fusion.5), channel_id=1, source_target_pairs={{0,2},{2,0},{4,6},{6,4},{8,10},{10,8},{12,14},{14,12},{16,18},{18,... | collective-permute-start | bytes 1544 | tf_op jit(solution)/shard_map/ppermute | solution.py:26
  229.7 6.2 %collective-permute-start.21 = (f32[4,16,2]{1,0,2:T(4,128)S(1)}, f32[4,16,2]{1,0,2:T(4,128)S(1)}, u32[]{:S(2)}, u32[]{:S(2)}) collective-permute-start(f32[4,16,2]{1,0,2:T(4,128)S(1)} %add_bitcast_fusion), channel_id=1, source_target_pairs={{0,1},{1,0},{2,3},{3,2},{4,5},{5,4},{6,7},{7,6},{8,9},{9,8},{10,11... | collective-permute-start | bytes 1544 | tf_op jit(solution)/shard_map/ppermute | solution.py:26
  235.8 5.3 %collective-permute-start.22 = (f32[4,16,2]{1,0,2:T(4,128)S(1)}, f32[4,16,2]{1,0,2:T(4,128)S(1)}, u32[]{:S(2)}, u32[]{:S(2)}) collective-permute-start(f32[4,16,2]{1,0,2:T(4,128)S(1)} %add.1242), channel_id=1, source_target_pairs={{0,64},{64,0},{128,192},{192,128},{1,65},{65,1},{129,193},{193,129... | collective-permute-start | bytes 1544 | tf_op jit(solution)/shard_map/ppermute | solution.py:26
  241.1 4.0 %collective-permute-start.23 = (f32[4,16,2]{1,0,2:T(4,128)S(1)}, f32[4,16,2]{1,0,2:T(4,128)S(1)}, u32[]{:S(2)}, u32[]{:S(2)}) collective-permute-start(f32[4,16,2]{1,0,2:T(4,128)S(1)} %add.1243), channel_id=1, source_target_pairs={{0,128},{64,192},{128,0},{192,64},{1,129},{65,193},{129,1},{193,65... | collective-permute-start | bytes 1544 | tf_op jit(solution)/shard_map/ppermute | solution.py:26
  (102 other events, 149.0 us)
